TPU v7x, 32 devices: a whole 2x2x4 slice. The times are simulated.
32 devices in a mesh: grp: 2 (over y), lat: 4 (over z), lon: 4 (over x, core).
Axes of the slice: x: 2, y: 2, z: 4, core: 2. Of those that a mesh axis runs over, the one named last changes fastest.
Arguments:
- inputs: bfloat16 [2, 16, 256, 256], P('grp', 'lat', 'lon'), parts along dimension 0, may hold values from -6 to 6
- cotangent: bfloat16 [2, 16, 256, 256], P('grp', 'lat', 'lon'), parts along dimension 0, may hold values from -6 to 6
- weight: bfloat16 [9, 256, 256], replicated, may hold values from -0.125 to 0.125
- src_rows: int32 [16, 12], replicated, may hold values from 0 to 15, as said below
- lon_start: int32 [16, 12], replicated, may hold values from -16 to 16, as said below
- lon_span: int32 [16, 12], replicated, may hold values from 1 to 256, as said below
- basis_idx: int32 [16, 12], replicated, may hold values from 0 to 8, as said below
- quad_weight: float32 [16, 12], replicated, may hold values from -4 to 4
Outputs:
- response: float32 [2, 16, 256, 256], P('grp', 'lat', 'lon'), parts along dimension 0
- grad_input: float32 [2, 16, 256, 256], P('grp', 'lat', 'lon'), parts along dimension 0
- grad_weight: float32 [18, 256, 256], P('grp', 'lat', 'lon'), parts along dimension 0
There are 2 independent parts, one for each index of `grp`. A program takes and returns all parts, laid end to end along the dimension named above; an argument that names none is the same for every part. Nothing has to cross between parts.
Inputs may be any that keep to these rules, and one draw needn't show every extreme that they name: `src_rows`: each entry's input row lies within 2 rows of its output row; every row has entries reaching exactly 2 rows up and down, clipped at the grid's edges. `lon_start`: for an entry with span 256 the start is 0; otherwise the range lies within 16 longitudes of the output longitude on either side. `lon_span`: either 256 (a full circle, only in the first and last 2 rows) or at most 33. `basis_idx`: every basis function appears in every row.
All inputs are finite; a program needn't handle non-finite values.
Results may differ from a plain program's by a relative error of at most 0.01.
Values may be sent and summed in bfloat16 or wider, within the bound.
No kernel may reach another device: no remote copies, remote signals or barrier semaphores. Data moves between devices by JAX's collectives and lax.ppermute only.
A program may use at most 64 MiB of HBM per device.

v0:
```python
import jax
import jax.numpy as jnp
from jax import lax
from jax.sharding import PartitionSpec as P

BASIS = 9
REACH = 2
RIM = 16


def with_halo(block, sides, width, periodic):
    for axis, dim in sides:
        count = lax.axis_size(axis)
        forward = [(i, i + 1) for i in range(count - 1)]
        if periodic:
            forward.append((count - 1, 0))
        backward = [(target, source) for source, target in forward]
        low = lax.ppermute(
            lax.slice_in_dim(block, block.shape[dim] - width, None, axis=dim), axis, forward
        )
        high = lax.ppermute(lax.slice_in_dim(block, 0, width, axis=dim), axis, backward)
        block = jnp.concatenate([low, block, high], axis=dim)
    return block


def lat_rim(grid_field):
    return with_halo(grid_field, (("lat", 1),), REACH, False)


def lon_rim(grid_field):
    return with_halo(grid_field, (("lon", 2),), RIM, True)


def extend(grid_field):
    return lon_rim(lat_rim(grid_field))


def cycle_totals(widened, lon_count):
    interior = lax.slice_in_dim(widened, RIM, RIM + lon_count, axis=2)
    return lax.psum(jnp.sum(interior, axis=2, dtype=jnp.float32), "lon")


def rows_share(partial_value):
    return lax.psum_scatter(partial_value, "lat", scatter_dimension=1, tiled=True)


def cols_share(partial_value):
    return lax.psum_scatter(partial_value, "lon", scatter_dimension=2, tiled=True)


def on_device(inputs, cotangent, weight, src_rows, lon_start, lon_span, basis_idx, quad_weight):
    members, row_count, lon_count, channels = inputs.shape
    lon_total = lon_count * lax.axis_size("lon")
    height = row_count * lax.axis_size("lat")
    first_row = lax.axis_index("lat") * row_count
    extent = lon_count + 2 * RIM
    weighting = quad_weight / jnp.sqrt(lon_span.astype(jnp.float32))
    basis_ids = jnp.arange(BASIS, dtype=jnp.int32)
    wide_cols = jnp.arange(extent, dtype=jnp.int32)[None, :, None] - RIM
    own_cols = jnp.arange(lon_count, dtype=jnp.int32)[None, None, :]
    widened = extend(inputs)
    totals = cycle_totals(widened, lon_count)

    def forward_row(position):
        out_row = first_row + position
        sources = lax.dynamic_index_in_dim(src_rows, out_row, 0, keepdims=False)
        starts = lax.dynamic_index_in_dim(lon_start, out_row, 0, keepdims=False)[:, None, None]
        spans = lax.dynamic_index_in_dim(lon_span, out_row, 0, keepdims=False)
        bases = lax.dynamic_index_in_dim(basis_idx, out_row, 0, keepdims=False)
        scales = lax.dynamic_index_in_dim(weighting, out_row, 0, keepdims=False)
        local_rows = sources - first_row + REACH
        offsets = wide_cols - own_cols
        span_cube = spans[:, None, None]
        banded = (
            (offsets >= starts) & (offsets < starts + span_cube) & (span_cube < lon_total)
        ).astype(jnp.bfloat16)
        picked = jnp.take(widened, local_rows, axis=1)
        boxed = jnp.einsum("bsvc,svw->bswc", picked, banded, preferred_element_type=jnp.float32)
        cycle_sum = jnp.take(totals, local_rows, axis=1)
        is_full = (spans == lon_total).astype(jnp.float32)
        boxed = boxed + is_full[None, :, None, None] * cycle_sum[:, :, None, :]
        mixing = scales[:, None] * (bases[:, None] == basis_ids[None, :]).astype(jnp.float32)
        return jnp.einsum("bswc,sk->bwkc", boxed, mixing).astype(jnp.bfloat16)

    filtered = lax.map(forward_row, jnp.arange(row_count, dtype=jnp.int32))
    flattened = filtered.reshape(row_count, members, lon_count, BASIS * channels)
    w_fwd = weight.reshape(BASIS * channels, channels)
    response = jnp.einsum("rbwq,qo->brwo", flattened, w_fwd, preferred_element_type=jnp.float32)
    grad_wide = extend(cotangent)
    grad_totals = cycle_totals(grad_wide, lon_count)
    pad_pair = ((REACH, REACH), (0, 0))
    window = row_count + 2 * REACH
    window_rows = 2 * REACH + 1
    pad_src = lax.dynamic_slice_in_dim(
        jnp.pad(src_rows, pad_pair, constant_values=-1), first_row, window, 0
    )
    pad_start = lax.dynamic_slice_in_dim(
        jnp.pad(lon_start, pad_pair, constant_values=0), first_row, window, 0
    )
    pad_span = lax.dynamic_slice_in_dim(
        jnp.pad(lon_span, pad_pair, constant_values=1), first_row, window, 0
    )
    pad_basis = lax.dynamic_slice_in_dim(
        jnp.pad(basis_idx, pad_pair, constant_values=0), first_row, window, 0
    )
    pad_scale = lax.dynamic_slice_in_dim(
        jnp.pad(weighting, pad_pair, constant_values=0.0), first_row, window, 0
    )
    back_offsets = (own_cols - wide_cols)[None]

    def backward_row(position):
        target = first_row + position
        grad_rows = lax.dynamic_slice_in_dim(grad_wide, position, window_rows, 1).astype(
            jnp.float32
        )
        cycle_rows = lax.dynamic_slice_in_dim(grad_totals, position, window_rows, 1)
        sources = lax.dynamic_slice_in_dim(pad_src, position, window_rows, 0)
        starts = lax.dynamic_slice_in_dim(pad_start, position, window_rows, 0)
        spans = lax.dynamic_slice_in_dim(pad_span, position, window_rows, 0)
        bases = lax.dynamic_slice_in_dim(pad_basis, position, window_rows, 0)
        scales = lax.dynamic_slice_in_dim(pad_scale, position, window_rows, 0)
        hits = (sources == target).astype(jnp.float32)
        picks = (bases[:, :, None] == basis_ids[None, None, :]).astype(jnp.float32)
        mixing = (scales * hits)[:, :, None] * picks
        start_cube = starts[:, :, None, None]
        span_cube = spans[:, :, None, None]
        banded = (
            (back_offsets >= start_cube)
            & (back_offsets < start_cube + span_cube)
            & (span_cube < lon_total)
        ).astype(jnp.float32)
        weighted_band = jnp.einsum(
            "esvw,esk->ekvw", banded, mixing, precision=lax.Precision.HIGHEST
        )
        local_part = jnp.einsum(
            "bevc,ekvw->bwkc", grad_rows, weighted_band, precision=lax.Precision.HIGHEST
        )
        full_mix = mixing * (spans == lon_total).astype(jnp.float32)[:, :, None]
        cycle_part = jnp.einsum(
            "bec,ek->bkc", cycle_rows, jnp.sum(full_mix, axis=1), precision=lax.Precision.HIGHEST
        )
        return (local_part + cycle_part[:, None, :, :]).astype(jnp.bfloat16)

    gathered_back = lax.map(backward_row, jnp.arange(row_count, dtype=jnp.int32))
    back_filtered = gathered_back.reshape(row_count, members, lon_count, BASIS * channels)
    w_back = jnp.transpose(weight, (0, 2, 1)).reshape(BASIS * channels, channels)
    grad_input = jnp.einsum(
        "rbwq,qc->brwc", back_filtered, w_back, preferred_element_type=jnp.float32
    )
    partial_value = jnp.einsum(
        "rbwq,brwo->qo", flattened, cotangent, preferred_element_type=jnp.float32
    )
    partial_value = partial_value.reshape(BASIS, channels, channels)
    reduced = rows_share(cols_share(partial_value))
    grad_weight = reduced / jnp.sqrt(jnp.float32(members * height * lon_total))
    return (response, grad_input, grad_weight)


def solution(mesh):
    placed = (
        P("grp", "lat", "lon", None),
        P("grp", "lat", "lon", None),
        P(),
        P(),
        P(),
        P(),
        P(),
        P(),
    )
    return jax.shard_map(
        on_device,
        mesh=mesh,
        in_specs=placed,
        out_specs=(
            P("grp", "lat", "lon", None),
            P("grp", "lat", "lon", None),
            P("grp", "lat", "lon"),
        ),
        check_vma=False,
    )
```

profile of v0, /device:TPU:0, one launch (start us, length us, event | category | flops | bytes accessed | tf_op | source)
XLA Modules:
  0.0 147.8 jit_solution(16851734251905731988)
XLA Ops:
  8.1 4.9 %collective-permute-start.4 = (bf16[1,2,64,256]{3,2,1,0:T(8,128)(2,1)S(1)}, bf16[1,2,64,256]{3,2,1,0:T(8,128)(2,1)S(1)}, u32[]{:S(2)}, u32[]{:S(2)}) collective-permute-start(bf16[1,2,64,256]{3,2,1,0:T(8,128)(2,1)S(1)} %get-tuple-element.480), channel_id=1, source_target_pairs={{0,4},{4,8},{8,12},{1,5},{5,9},{9,13},{2,6},{6,10},{10,14},{3,7},{... | collective-permute-start | bytes 196616 | tf_op jit(solution)/shard_map/ppermute | solution.py:18
  15.3 4.5 %collective-permute-start = (bf16[1,2,64,256]{3,2,1,0:T(8,128)(2,1)S(1)}, bf16[1,2,64,256]{3,2,1,0:T(8,128)(2,1)S(1)}, u32[]{:S(2)}, u32[]{:S(2)}) collective-permute-start(bf16[1,2,64,256]{3,2,1,0:T(8,128)(2,1)S(1)} %get-tuple-element.482), channel_id=1, source_target_pairs={{0,4},{4,8},{8,12},{1,5},{5,9},{9,13},{2,6},{6,10},{10,14},{3,7},{... | collective-permute-start | bytes 196616 | tf_op jit(solution)/shard_map/ppermute | solution.py:18
  23.4 2.6 %collective-permute-done.1 = bf16[1,2,64,256]{3,2,1,0:T(8,128)(2,1)S(1)} collective-permute-done((bf16[1,2,64,256]{3,2,1,0:T(8,128)(2,1)S(1)}, bf16[1,2,64,256]{3,2,1,0:T(8,128)(2,1)S(1)}, u32[]{:S(2)}, u32[]{:S(2)}) %collective-permute-start.1) | collective-permute-done | bytes 65568 | tf_op jit(solution)/shard_map/ppermute | solution.py:21
  26.1 1.7 %collective-permute-start.3 = (bf16[1,8,16,256]{3,2,1,0:T(8,128)(2,1)S(1)}, bf16[1,8,16,256]{3,2,1,0:T(8,128)(2,1)S(1)}, u32[]{:S(2)}, u32[]{:S(2)}) collective-permute-start(bf16[1,8,16,256]{3,2,1,0:T(8,128)(2,1)S(1)} %get-tuple-element.478), channel_id=1, source_target_pairs={{1,0},{2,1},{3,2},{0,3},{5,4},{6,5},{7,6},{4,7},{9,8},{10,9},{11,1... | collective-permute-start | bytes 196616 | tf_op jit(solution)/shard_map/ppermute | solution.py:21
  28.0 10.1 %all-reduce.5 = (f32[1,8,256]{2,1,0:T(8,128)S(1)}, f32[1,8,256]{2,1,0:T(8,128)S(1)}) all-reduce(f32[1,8,256]{2,1,0:T(8,128)S(1)} %bitcast.167, f32[1,8,256]{2,1,0:T(8,128)S(1)} %bitcast.168), channel_id=1, replica_groups=mesh['grp'=2,'lat'=4,'lon'=4] {'lon'}, use_global_device_ids=true, to_apply=%region_1.0 | all-reduce | flops 4096 | bytes 32768 | tf_op jit(solution)/shard_map/psum | solution.py:40
  38.2 23.8 %while.26 = (s32[]{:T(128)}, bf16[4,1,64,9,256]{4,3,2,1,0:T(8,128)(2,1)S(1)}, s32[4]{0:T(128)S(1)}, s32[]{:T(128)}, s32[16,12]{1,0:T(8,128)}, /*index=5*/bf16[16...) while((s32[]{:T(128)}, ...), condition=%wide.region_3.4_spmd.clone.clone, body=%wide.region_2.3_spmd.clone.clone.sunk | while | flops 42284552 | bytes 3197819 | solution.py:85
  62.7 2.8 %convolution_bitcast_fusion = f32[9,256,256]{1,2,0:T(8,128)} fusion(bf16[4,8,9,8,256]{4,3,2,1,0:T(8,128)(2,1)S(1)} %bitcast.162, bf16[1,4,64,256]{3,2,1,0:T(8,128)(2,1)} %param.13), kind=kOutput, calls=%fused_computation.91 | convolution fusion | flops 301989888 | bytes 3670016 | tf_op jit(solution)/shard_map/rbwq,brwo->qo/dot_general | solution.py:150
  66.8 1.6 %copy.22 = bf16[9,256,256]{1,2,0:T(8,128)(2,1)} copy(bf16[9,256,256]{2,1,0:T(8,128)(2,1)S(1)} %copy-done.2) | data formatting | bytes 2359296 | tf_op args[2]
  68.6 1.7 %collective-permute-start.7 = (bf16[1,8,16,256]{3,2,1,0:T(8,128)(2,1)S(1)}, bf16[1,8,16,256]{3,2,1,0:T(8,128)(2,1)S(1)}, u32[]{:S(2)}, u32[]{:S(2)}) collective-permute-start(bf16[1,8,16,256]{3,2,1,0:T(8,128)(2,1)S(1)} %get-tuple-element.476), channel_id=1, source_target_pairs={{1,0},{2,1},{3,2},{0,3},{5,4},{6,5},{7,6},{4,7},{9,8},{10,9},{11,1... | collective-permute-start | bytes 196616 | tf_op jit(solution)/shard_map/ppermute | solution.py:21
  70.3 1.9 %collective-permute-done.6 = bf16[1,8,16,256]{3,2,1,0:T(8,128)(2,1)S(1)} collective-permute-done((bf16[1,8,16,256]{3,2,1,0:T(8,128)(2,1)S(1)}, bf16[1,8,16,256]{3,2,1,0:T(8,128)(2,1)S(1)}, u32[]{:S(2)}, u32[]{:S(2)}) %collective-permute-start.6) | collective-permute-done | bytes 65568 | tf_op jit(solution)/shard_map/ppermute | solution.py:18
  73.1 26.1 %reduce-scatter.5.cloned.1.call-done = f32[9,256,64]{1,2,0:T(8,128)} async-done(((f32[9,256,256]{1,2,0:T(8,128)}), f32[9,256,64]{1,2,0:T(8,128)}) %reduce-scatter.5.cloned.1.call-update) | async-done | bytes 589840 | tf_op jit(solution)/shard_map/reduce_scatter | solution.py:48
  99.1 2.4 %copy.28 = f32[9,256,64]{2,0,1:T(8,128)S(1)} copy(f32[9,256,64]{1,2,0:T(8,128)} %reduce-scatter.5.cloned.1.call-done) | data formatting | bytes 1179648
  102.8 28.7 %while.27 = (s32[]{:T(128)}, bf16[4,1,64,9,256]{4,2,3,1,0:T(8,128)(2,1)}, s32[4]{0:T(128)S(1)}, s32[8,12]{1,0:T(8,128)S(1)}, s32[8,12]{1,0:T(8,128)S(1)}, /*inde...) while((s32[]{:T(128)}, ...), condition=%wide.region_8.9_spmd.clone.clone, body=%wide.region_6.8_spmd.clone.clone.sunk | while | flops 891077120 | bytes 5929787 | solution.py:144
  106.1 1.6 %fusion.122 = f32[5,9,96,64]{2,1,3,0:T(8,128)S(1)} fusion(s32[5,12]{1,0:T(8,128)S(1)} %get-tuple-element.642, s32[5,12]{1,0:T(8,128)S(1)} %get-tuple-element.643, s32[96,64]{0,1:T(8,128)S(1)} %subtract_bitcast_fusion.2, pred[5,12]{1,0:T(8,128)(4,1)S(1)} %get-tuple-element.644, f32[5,12]{1,0:T(8,128)S(1)} %dynamic-slice_select_fusion.2, ...), kind=kOutput, calls=%fused_computation.52.clone.1 | convolution fusion | flops 41288760 | bytes 1131516 | tf_op jit(solution)/shard_map/while/body/eval_jaxpr/esvw,esk->ekvw/dot_general | solution.py:132
  108.0 2.0 %fusion.125 = bf16[4,1,64,9,256]{4,2,3,1,0:T(8,128)(2,1)} fusion(bf16[4,1,64,9,256]{4,2,3,1,0:T(8,128)(2,1)} %get-tuple-element.705, s32[]{:T(128)} %get-tuple-element.704, f32[5,9,96,64]{2,1,3,0:T(8,128)S(1)} %fusion.122, f32[9,256]{1,0:T(8,128)S(1)} %fusion.124, bf16[1,8,96,256]{3,2,1,0:T(8,128)(2,1)S(1)} %copy-done, s32[]{:T(128)S(6)} %select_n.107), kind=kOutput, calls=%fused_computation.67.clone.1 | convolution fusion | flops 849641472 | bytes 3179012 | tf_op jit(solution)/shard_map/while/body/eval_jaxpr/bevc,ekvw->bwkc/dot_general | solution.py:135
  113.2 1.6 %fusion.122 = f32[5,9,96,64]{2,1,3,0:T(8,128)S(1)} fusion(s32[5,12]{1,0:T(8,128)S(1)} %get-tuple-element.642, s32[5,12]{1,0:T(8,128)S(1)} %get-tuple-element.643, s32[96,64]{0,1:T(8,128)S(1)} %subtract_bitcast_fusion.2, pred[5,12]{1,0:T(8,128)(4,1)S(1)} %get-tuple-element.644, f32[5,12]{1,0:T(8,128)S(1)} %dynamic-slice_select_fusion.2, ...), kind=kOutput, calls=%fused_computation.52.clone.1 | convolution fusion | flops 41288760 | bytes 1131516 | tf_op jit(solution)/shard_map/while/body/eval_jaxpr/esvw,esk->ekvw/dot_general | solution.py:132
  115.1 2.0 %fusion.125 = bf16[4,1,64,9,256]{4,2,3,1,0:T(8,128)(2,1)} fusion(bf16[4,1,64,9,256]{4,2,3,1,0:T(8,128)(2,1)} %get-tuple-element.705, s32[]{:T(128)} %get-tuple-element.704, f32[5,9,96,64]{2,1,3,0:T(8,128)S(1)} %fusion.122, f32[9,256]{1,0:T(8,128)S(1)} %fusion.124, bf16[1,8,96,256]{3,2,1,0:T(8,128)(2,1)S(1)} %copy-done, s32[]{:T(128)S(6)} %select_n.107), kind=kOutput, calls=%fused_computation.67.clone.1 | convolution fusion | flops 849641472 | bytes 3179012 | tf_op jit(solution)/shard_map/while/body/eval_jaxpr/bevc,ekvw->bwkc/dot_general | solution.py:135
  120.4 1.6 %fusion.122 = f32[5,9,96,64]{2,1,3,0:T(8,128)S(1)} fusion(s32[5,12]{1,0:T(8,128)S(1)} %get-tuple-element.642, s32[5,12]{1,0:T(8,128)S(1)} %get-tuple-element.643, s32[96,64]{0,1:T(8,128)S(1)} %subtract_bitcast_fusion.2, pred[5,12]{1,0:T(8,128)(4,1)S(1)} %get-tuple-element.644, f32[5,12]{1,0:T(8,128)S(1)} %dynamic-slice_select_fusion.2, ...), kind=kOutput, calls=%fused_computation.52.clone.1 | convolution fusion | flops 41288760 | bytes 1131516 | tf_op jit(solution)/shard_map/while/body/eval_jaxpr/esvw,esk->ekvw/dot_general | solution.py:132
  122.3 2.0 %fusion.125 = bf16[4,1,64,9,256]{4,2,3,1,0:T(8,128)(2,1)} fusion(bf16[4,1,64,9,256]{4,2,3,1,0:T(8,128)(2,1)} %get-tuple-element.705, s32[]{:T(128)} %get-tuple-element.704, f32[5,9,96,64]{2,1,3,0:T(8,128)S(1)} %fusion.122, f32[9,256]{1,0:T(8,128)S(1)} %fusion.124, bf16[1,8,96,256]{3,2,1,0:T(8,128)(2,1)S(1)} %copy-done, s32[]{:T(128)S(6)} %select_n.107), kind=kOutput, calls=%fused_computation.67.clone.1 | convolution fusion | flops 849641472 | bytes 3179012 | tf_op jit(solution)/shard_map/while/body/eval_jaxpr/bevc,ekvw->bwkc/dot_general | solution.py:135
  127.5 1.6 %fusion.122 = f32[5,9,96,64]{2,1,3,0:T(8,128)S(1)} fusion(s32[5,12]{1,0:T(8,128)S(1)} %get-tuple-element.642, s32[5,12]{1,0:T(8,128)S(1)} %get-tuple-element.643, s32[96,64]{0,1:T(8,128)S(1)} %subtract_bitcast_fusion.2, pred[5,12]{1,0:T(8,128)(4,1)S(1)} %get-tuple-element.644, f32[5,12]{1,0:T(8,128)S(1)} %dynamic-slice_select_fusion.2, ...), kind=kOutput, calls=%fused_computation.52.clone.1 | convolution fusion | flops 41288760 | bytes 1131516 | tf_op jit(solution)/shard_map/while/body/eval_jaxpr/esvw,esk->ekvw/dot_general | solution.py:132
  129.4 2.0 %fusion.125 = bf16[4,1,64,9,256]{4,2,3,1,0:T(8,128)(2,1)} fusion(bf16[4,1,64,9,256]{4,2,3,1,0:T(8,128)(2,1)} %get-tuple-element.705, s32[]{:T(128)} %get-tuple-element.704, f32[5,9,96,64]{2,1,3,0:T(8,128)S(1)} %fusion.122, f32[9,256]{1,0:T(8,128)S(1)} %fusion.124, bf16[1,8,96,256]{3,2,1,0:T(8,128)(2,1)S(1)} %copy-done, s32[]{:T(128)S(6)} %select_n.107), kind=kOutput, calls=%fused_computation.67.clone.1 | convolution fusion | flops 849641472 | bytes 3179012 | tf_op jit(solution)/shard_map/while/body/eval_jaxpr/bevc,ekvw->bwkc/dot_general | solution.py:135
  131.4 2.0 %copy.21 = bf16[4,1,64,9,256]{4,3,2,0,1:T(8,128)(2,1)S(1)} copy(bf16[4,1,64,9,256]{4,2,3,1,0:T(8,128)(2,1)} %get-tuple-element.253) | data formatting | bytes 2359296 | tf_op jit(solution)/shard_map/while | solution.py:144
  133.5 1.6 %reshape.372 = bf16[4,64,2304]{2,1,0:T(8,128)(2,1)} reshape(bf16[4,1,64,9,256]{4,3,2,0,1:T(8,128)(2,1)S(1)} %copy.21) | data formatting | bytes 2359296 | tf_op jit(solution)/shard_map/reshape.32
  135.0 2.6 %convolution_bitcast_fusion.2 = f32[1,4,64,256]{3,2,1,0:T(8,128)} fusion(bf16[4,64,2304]{2,1,0:T(8,128)(2,1)S(1)} %reshape.370, bf16[2304,256,1]{1,0,2:T(8,128)(2,1)} %bitcast.164), kind=kOutput, calls=%fused_computation.95 | convolution fusion | flops 301989888 | bytes 2621440 | tf_op jit(solution)/shard_map/rbwq,qo->brwo/dot_general | solution.py:88
  (155 shorter events, 39.4 us)
Async XLA Ops:
  7.2 20.7 %copy-start.4 = (bf16[1,4,64,256]{3,2,1,0:T(8,128)(2,1)S(1)}, bf16[1,4,64,256]{3,2,1,0:T(8,128)(2,1)}, u32[]{:S(2)}) copy-start(bf16[1,4,64,256]{3,2,1,0:T(8,128)(2,1)} %param.13) | copy-start | bytes 393220
  7.2 92.0 %reduce-scatter.5.cloned.1.call-start = ((), (), s32[]{:S(2)}) async-start(), calls=%async_computation.2 | async-start | bytes 2949120 | tf_op jit(solution)/shard_map/reduce_scatter | solution.py:48
  8.1 19.7 %collective-permute-start.4 = (bf16[1,2,64,256]{3,2,1,0:T(8,128)(2,1)S(1)}, bf16[1,2,64,256]{3,2,1,0:T(8,128)(2,1)S(1)}, u32[]{:S(2)}, u32[]{:S(2)}) collective-permute-start(bf16[1,2,64,256]{3,2,1,0:T(8,128)(2,1)S(1)} %get-tuple-element.480), channel_id=1, source_target_pairs={{0,4},{4,8},{8,12},{1,5},{5,9},{9,13},{2,6},{6,10},{10,14},{3,7},{... | collective-permute-start | bytes 196616 | tf_op jit(solution)/shard_map/ppermute | solution.py:18
  13.1 14.8 %collective-permute-start.5 = (bf16[1,2,64,256]{3,2,1,0:T(8,128)(2,1)S(1)}, bf16[1,2,64,256]{3,2,1,0:T(8,128)(2,1)S(1)}, u32[]{:S(2)}, u32[]{:S(2)}) collective-permute-start(bf16[1,2,64,256]{3,2,1,0:T(8,128)(2,1)S(1)} %get-tuple-element.479), channel_id=1, source_target_pairs={{4,0},{8,4},{12,8},{5,1},{9,5},{13,9},{6,2},{10,6},{14,10},{7,3},{... | collective-permute-start | bytes 196616 | tf_op jit(solution)/shard_map/ppermute | solution.py:21
  15.3 7.2 %collective-permute-start = (bf16[1,2,64,256]{3,2,1,0:T(8,128)(2,1)S(1)}, bf16[1,2,64,256]{3,2,1,0:T(8,128)(2,1)S(1)}, u32[]{:S(2)}, u32[]{:S(2)}) collective-permute-start(bf16[1,2,64,256]{3,2,1,0:T(8,128)(2,1)S(1)} %get-tuple-element.482), channel_id=1, source_target_pairs={{0,4},{4,8},{8,12},{1,5},{5,9},{9,13},{2,6},{6,10},{10,14},{3,7},{... | collective-permute-start | bytes 196616 | tf_op jit(solution)/shard_map/ppermute | solution.py:18
  19.8 6.2 %collective-permute-start.1 = (bf16[1,2,64,256]{3,2,1,0:T(8,128)(2,1)S(1)}, bf16[1,2,64,256]{3,2,1,0:T(8,128)(2,1)S(1)}, u32[]{:S(2)}, u32[]{:S(2)}) collective-permute-start(bf16[1,2,64,256]{3,2,1,0:T(8,128)(2,1)S(1)} %get-tuple-element.481), channel_id=1, source_target_pairs={{4,0},{8,4},{12,8},{5,1},{9,5},{13,9},{6,2},{10,6},{14,10},{7,3},{... | collective-permute-start | bytes 196616 | tf_op jit(solution)/shard_map/ppermute | solution.py:21
  23.4 14.8 %copy-start.5 = (s32[16,12]{1,0:T(8,128)S(1)}, s32[16,12]{1,0:T(8,128)}, u32[]{:S(2)}) copy-start(s32[16,12]{1,0:T(8,128)} %param.17) | copy-start | bytes 2308
  26.0 12.1 %collective-permute-start.2 = (bf16[1,8,16,256]{3,2,1,0:T(8,128)(2,1)S(1)}, bf16[1,8,16,256]{3,2,1,0:T(8,128)(2,1)S(1)}, u32[]{:S(2)}, u32[]{:S(2)}) collective-permute-start(bf16[1,8,16,256]{3,2,1,0:T(8,128)(2,1)S(1)} %get-tuple-element.477), channel_id=1, source_target_pairs={{0,1},{1,2},{2,3},{3,0},{4,5},{5,6},{6,7},{7,4},{8,9},{9,10},{10,1... | collective-permute-start | bytes 196616 | tf_op jit(solution)/shard_map/ppermute | solution.py:18
  26.1 12.1 %collective-permute-start.3 = (bf16[1,8,16,256]{3,2,1,0:T(8,128)(2,1)S(1)}, bf16[1,8,16,256]{3,2,1,0:T(8,128)(2,1)S(1)}, u32[]{:S(2)}, u32[]{:S(2)}) collective-permute-start(bf16[1,8,16,256]{3,2,1,0:T(8,128)(2,1)S(1)} %get-tuple-element.478), channel_id=1, source_target_pairs={{1,0},{2,1},{3,2},{0,3},{5,4},{6,5},{7,6},{4,7},{9,8},{10,9},{11,1... | collective-permute-start | bytes 196616 | tf_op jit(solution)/shard_map/ppermute | solution.py:21
  65.6 1.3 copy-start.2
  65.6 73.2 %reduce-scatter.7.cloned.1.call-start = ((), (), s32[]{:S(2)}) async-start(), calls=%async_computation.3 | async-start | bytes 819200
  66.8 1.6 %copy-start.6 = (f32[16,12]{1,0:T(8,128)S(1)}, f32[16,12]{1,0:T(8,128)}, u32[]{:S(2)}) copy-start(f32[16,12]{1,0:T(8,128)} %get-tuple-element.466) | copy-start | bytes 2308
  66.8 1.6 %copy-start.7 = (s32[16,12]{1,0:T(8,128)S(1)}, s32[16,12]{1,0:T(8,128)}, u32[]{:S(2)}) copy-start(s32[16,12]{1,0:T(8,128)} %get-tuple-element.759) | copy-start | bytes 2308
  66.8 1.6 %copy-start.9 = (s32[16,12]{1,0:T(8,128)S(1)}, s32[16,12]{1,0:T(8,128)}, u32[]{:S(2)}) copy-start(s32[16,12]{1,0:T(8,128)} %get-tuple-element.761) | copy-start | bytes 2308
  66.8 1.6 %copy-start.8 = (s32[16,12]{1,0:T(8,128)S(1)}, s32[16,12]{1,0:T(8,128)}, u32[]{:S(2)}) copy-start(s32[16,12]{1,0:T(8,128)} %get-tuple-element.760) | copy-start | bytes 2308
  68.5 3.7 %collective-permute-start.6 = (bf16[1,8,16,256]{3,2,1,0:T(8,128)(2,1)S(1)}, bf16[1,8,16,256]{3,2,1,0:T(8,128)(2,1)S(1)}, u32[]{:S(2)}, u32[]{:S(2)}) collective-permute-start(bf16[1,8,16,256]{3,2,1,0:T(8,128)(2,1)S(1)} %get-tuple-element.475), channel_id=1, source_target_pairs={{0,1},{1,2},{2,3},{3,0},{4,5},{5,6},{6,7},{7,4},{8,9},{9,10},{10,1... | collective-permute-start | bytes 196616 | tf_op jit(solution)/shard_map/ppermute | solution.py:18
  68.6 3.7 %collective-permute-start.7 = (bf16[1,8,16,256]{3,2,1,0:T(8,128)(2,1)S(1)}, bf16[1,8,16,256]{3,2,1,0:T(8,128)(2,1)S(1)}, u32[]{:S(2)}, u32[]{:S(2)}) collective-permute-start(bf16[1,8,16,256]{3,2,1,0:T(8,128)(2,1)S(1)} %get-tuple-element.476), channel_id=1, source_target_pairs={{1,0},{2,1},{3,2},{0,3},{5,4},{6,5},{7,6},{4,7},{9,8},{10,9},{11,1... | collective-permute-start | bytes 196616 | tf_op jit(solution)/shard_map/ppermute | solution.py:21
  106.0 1.9 %copy-start = (bf16[1,8,96,256]{3,2,1,0:T(8,128)(2,1)S(1)}, bf16[1,8,96,256]{3,2,1,0:T(8,128)(2,1)}, u32[]{:S(2)}) copy-start(bf16[1,8,96,256]{3,2,1,0:T(8,128)(2,1)} %get-tuple-element.728) | copy-start | bytes 1179652 | tf_op jit(solution)/shard_map/while
  113.2 1.9 %copy-start = (bf16[1,8,96,256]{3,2,1,0:T(8,128)(2,1)S(1)}, bf16[1,8,96,256]{3,2,1,0:T(8,128)(2,1)}, u32[]{:S(2)}) copy-start(bf16[1,8,96,256]{3,2,1,0:T(8,128)(2,1)} %get-tuple-element.728) | copy-start | bytes 1179652 | tf_op jit(solution)/shard_map/while
  120.4 1.9 %copy-start = (bf16[1,8,96,256]{3,2,1,0:T(8,128)(2,1)S(1)}, bf16[1,8,96,256]{3,2,1,0:T(8,128)(2,1)}, u32[]{:S(2)}) copy-start(bf16[1,8,96,256]{3,2,1,0:T(8,128)(2,1)} %get-tuple-element.728) | copy-start | bytes 1179652 | tf_op jit(solution)/shard_map/while
  127.5 1.9 %copy-start = (bf16[1,8,96,256]{3,2,1,0:T(8,128)(2,1)S(1)}, bf16[1,8,96,256]{3,2,1,0:T(8,128)(2,1)}, u32[]{:S(2)}) copy-start(bf16[1,8,96,256]{3,2,1,0:T(8,128)(2,1)} %get-tuple-element.728) | copy-start | bytes 1179652 | tf_op jit(solution)/shard_map/while
  135.0 2.6 %copy-start.1 = (bf16[4,64,2304]{2,1,0:T(8,128)(2,1)S(1)}, bf16[4,64,2304]{2,1,0:T(8,128)(2,1)}, u32[]{:S(2)}) copy-start(bf16[4,64,2304]{2,1,0:T(8,128)(2,1)} %reshape.372) | copy-start | bytes 3538948
  135.0 2.6 %copy-start.3 = (bf16[9,256,256]{1,2,0:T(8,128)(2,1)S(1)}, bf16[9,256,256]{1,2,0:T(8,128)(2,1)}, u32[]{:S(2)}) copy-start(bf16[9,256,256]{1,2,0:T(8,128)(2,1)} %copy.22) | copy-start | bytes 3538948
Sparse Core Ops, SparseCore 0:
  65.7 33.3 reduce-scatter.4
  102.9 22.2 reduce-scatter.6
where the time goes:
time: 149 us; the launch traced here: 148 us
  waiting for transfers between devices  30.7 us (21%)
  local copies, waits for them, and re-layouts  27.7 us (19%)
  matrix products  24.5 us (16%)
  starting transfers between devices  15.7 us (11%)
  between operations  14.3 us (10%)
  loops' own time  13.1 us (9%)
  other arithmetic  11.6 us (8%)
  blocking collectives  10.1 us (7%)
    reduce_scatter x1, waiting for transfers between devices, cols_share(): lax.psum_scatter(partial_value, 'lon', scatter_dimension=2, tiled=True)  26.1 us
    another operation x1, loops' own time, on_device(): lax.map(backward_row, jnp.arange(row_count, dtype=jnp.int32))  10.6 us
    psum x1, blocking collectives, cycle_totals(): return lax.psum(jnp.sum(interior, axis=2, dtype=jnp.float32), 'lon')  10.1 us
    ppermute x4, starting transfers between devices, with_halo(): lax.ppermute(lax.slice_in_dim(block, block.shape[dim] - width, None, axis...  9.59 us
    unnamed x28, local copies, waits for them, and re-layouts  9.4 us
    dot_general x4, matrix products, backward_row(): jnp.einsum('bevc,ekvw->bwkc', grad_rows, weighted_band, precision=lax.Pre...  8.02 us
    dot_general x4, matrix products, backward_row(): jnp.einsum('esvw,esk->ekvw', banded, mixing, precision=lax.Precision.HIGH...  6.34 us
    ppermute x4, starting transfers between devices, with_halo(): lax.ppermute(lax.slice_in_dim(block, 0, width, axis=dim), axis, backward)  6.05 us
  transfers between devices with their start and end apart: 10, of which 3 were waited for; matrix products, arithmetic and copies ran while one was open for 21% of the time, Pallas kernels for 0%

commit v1 on v0

--- a/solution.py
+++ b/solution.py
@@ -37,7 +37,7 @@
 
 def cycle_totals(widened, lon_count):
     interior = lax.slice_in_dim(widened, RIM, RIM + lon_count, axis=2)
-    return lax.psum(jnp.sum(interior, axis=2, dtype=jnp.float32), "lon")
+    return jnp.sum(lax.all_gather(jnp.sum(interior, axis=2, dtype=jnp.float32), "lon"), axis=0)
 
 
 def rows_share(partial_value):

time: 149 us -> 125 us (0.84)
  other arithmetic: 11.6 us -> 2.75 us
  waiting for transfers between devices: 30.7 us -> 22.2 us
  local copies, waits for them, and re-layouts: 27.7 us -> 23 us
    all_gather x0 -> x2, blocking collectives: none -> 10.4 us  [cycle_totals(): lax.all_gather(jnp.sum(interior, axis=2, dtype=jnp.float32), 'lon')]
    reduce_scatter x1, waiting for transfers between devices: 26.1 us -> 15.7 us  [cols_share(): lax.psum_scatter(partial_value, 'lon', scatter_dimension=2, tiled=True)]
    psum x1 -> x0, blocking collectives: 10.1 us -> none  [cycle_totals(): return lax.psum(jnp.sum(interior, axis=2, dtype=jnp.float32), 'lon')]
    ppermute x4, waiting for transfers between devices: 2.6 us -> 6.41 us  [with_halo(): lax.ppermute(lax.slice_in_dim(block, 0, width, axis=dim), axis, backward)]
    add x4, other arithmetic: 2.8 us -> 0.06 us  [forward_row(): starts + span_cube]
    select_n x4, other arithmetic: 2.8 us -> 0.06 us  [forward_row(): picked = jnp.take(widened, local_rows, axis=1)]
    lt x4, other arithmetic: 2.81 us -> 0.07 us  [forward_row(): span_cube < lon_total]
    eq x4, local copies, waits for them, and re-layouts: 2.79 us -> 0.05 us  [forward_row(): bases[:, None] == basis_ids[None, :]]
  transfers between devices with their start and end apart: 10 -> 10, of which waited for: 3 -> 3; matrix products, arithmetic and copies ran while one was open for 21% -> 24% of each run, Pallas kernels for 0% -> 0%
where the time goes in v1:
time: 125 us
  matrix products  23.7 us (19%)
  local copies, waits for them, and re-layouts  23 us (18%)
  waiting for transfers between devices  22.2 us (18%)
  starting transfers between devices  14.8 us (12%)
  between operations  14.4 us (12%)
  loops' own time  13.6 us (11%)
  blocking collectives  10.4 us (8%)
  other arithmetic  2.75 us (2%)
    reduce_scatter x1, waiting for transfers between devices, cols_share(): lax.psum_scatter(partial_value, 'lon', scatter_dimension=2, tiled=True)  15.7 us
    another operation x1, loops' own time, on_device(): lax.map(backward_row, jnp.arange(row_count, dtype=jnp.int32))  10.6 us
    all_gather x2, blocking collectives, cycle_totals(): lax.all_gather(jnp.sum(interior, axis=2, dtype=jnp.float32), 'lon')  10.4 us
    ppermute x4, starting transfers between devices, with_halo(): lax.ppermute(lax.slice_in_dim(block, block.shape[dim] - width, None, axis...  8.66 us
    unnamed x26, local copies, waits for them, and re-layouts  8.37 us
    dot_general x4, matrix products, backward_row(): jnp.einsum('bevc,ekvw->bwkc', grad_rows, weighted_band, precision=lax.Pre...  8.01 us
    ppermute x4, waiting for transfers between devices, with_halo(): lax.ppermute(lax.slice_in_dim(block, 0, width, axis=dim), axis, backward)  6.41 us
    dot_general x4, matrix products, backward_row(): jnp.einsum('esvw,esk->ekvw', banded, mixing, precision=lax.Precision.HIGH...  6.39 us
  transfers between devices with their start and end apart: 10, of which 3 were waited for; matrix products, arithmetic and copies ran while one was open for 24% of the time, Pallas kernels for 0%

profile of v1, /device:TPU:0, one launch (start us, length us, event | category | flops | bytes accessed | tf_op | source)
XLA Modules:
  0.0 124.8 jit_solution(6024290676151284183)
XLA Ops:
  8.1 4.9 %collective-permute-start = (bf16[1,2,64,256]{3,2,1,0:T(8,128)(2,1)S(1)}, bf16[1,2,64,256]{3,2,1,0:T(8,128)(2,1)S(1)}, u32[]{:S(2)}, u32[]{:S(2)}) collective-permute-start(bf16[1,2,64,256]{3,2,1,0:T(8,128)(2,1)S(1)} %get-tuple-element.494), channel_id=1, source_target_pairs={{0,4},{4,8},{8,12},{1,5},{5,9},{9,13},{2,6},{6,10},{10,14},{3,7},{... | collective-permute-start | bytes 196616 | tf_op jit(solution)/shard_map/ppermute | solution.py:18
  16.0 3.2 %collective-permute-done.1 = bf16[1,2,64,256]{3,2,1,0:T(8,128)(2,1)S(1)} collective-permute-done((bf16[1,2,64,256]{3,2,1,0:T(8,128)(2,1)S(1)}, bf16[1,2,64,256]{3,2,1,0:T(8,128)(2,1)S(1)}, u32[]{:S(2)}, u32[]{:S(2)}) %collective-permute-start.1) | collective-permute-done | bytes 65568 | tf_op jit(solution)/shard_map/ppermute | solution.py:21
  19.4 1.7 %collective-permute-start.3 = (bf16[1,8,16,256]{3,2,1,0:T(8,128)(2,1)S(1)}, bf16[1,8,16,256]{3,2,1,0:T(8,128)(2,1)S(1)}, u32[]{:S(2)}, u32[]{:S(2)}) collective-permute-start(bf16[1,8,16,256]{3,2,1,0:T(8,128)(2,1)S(1)} %get-tuple-element.490), channel_id=1, source_target_pairs={{1,0},{2,1},{3,2},{0,3},{5,4},{6,5},{7,6},{4,7},{9,8},{10,9},{11,1... | collective-permute-start | bytes 196616 | tf_op jit(solution)/shard_map/ppermute | solution.py:21
  21.1 5.2 %all-gather = f32[32,256]{1,0:T(8,128)S(1)} all-gather(f32[8,256]{1,0:T(8,128)S(1)} %convert_reduce_fusion.1), channel_id=2, replica_groups=mesh['grp'=2,'lat'=4,'lon'=4] {'lon'}, dimensions={0}, use_global_device_ids=true | all-gather | bytes 40960 | tf_op jit(solution)/shard_map/all_gather | solution.py:40
  26.4 13.4 %while.26 = (s32[]{:T(128)}, bf16[4,1,64,9,256]{4,3,2,1,0:T(8,128)(2,1)S(1)}, s32[4]{0:T(128)S(1)}, s32[]{:T(128)}, s32[16,12]{1,0:T(8,128)S(1)}, /*index=5*/bf1...) while((s32[]{:T(128)}, ...), condition=%wide.region_3.4_spmd.clone.clone, body=%wide.region_2.3_spmd.clone.clone.sunk | while | flops 42284552 | bytes 3197819 | solution.py:85
  40.7 1.9 %convolution_bitcast_fusion = f32[9,256,256]{1,2,0:T(8,128)} fusion(bf16[4,8,9,8,256]{4,3,2,1,0:T(8,128)(2,1)S(1)} %bitcast.167, bf16[1,4,64,256]{3,2,1,0:T(8,128)(2,1)S(1)} %copy-done.4), kind=kOutput, calls=%fused_computation.91 | convolution fusion | flops 301989888 | bytes 3670016 | tf_op jit(solution)/shard_map/rbwq,brwo->qo/dot_general | solution.py:150
  42.7 3.6 %collective-permute-start.4 = (bf16[1,2,64,256]{3,2,1,0:T(8,128)(2,1)S(1)}, bf16[1,2,64,256]{3,2,1,0:T(8,128)(2,1)S(1)}, u32[]{:S(2)}, u32[]{:S(2)}) collective-permute-start(bf16[1,2,64,256]{3,2,1,0:T(8,128)(2,1)S(1)} %get-tuple-element.492), channel_id=1, source_target_pairs={{0,4},{4,8},{8,12},{1,5},{5,9},{9,13},{2,6},{6,10},{10,14},{3,7},{... | collective-permute-start | bytes 196616 | tf_op jit(solution)/shard_map/ppermute | solution.py:18
  49.3 3.2 %collective-permute-done.5 = bf16[1,2,64,256]{3,2,1,0:T(8,128)(2,1)S(1)} collective-permute-done((bf16[1,2,64,256]{3,2,1,0:T(8,128)(2,1)S(1)}, bf16[1,2,64,256]{3,2,1,0:T(8,128)(2,1)S(1)}, u32[]{:S(2)}, u32[]{:S(2)}) %collective-permute-start.5) | collective-permute-done | bytes 65568 | tf_op jit(solution)/shard_map/ppermute | solution.py:21
  52.6 1.7 %collective-permute-start.7 = (bf16[1,8,16,256]{3,2,1,0:T(8,128)(2,1)S(1)}, bf16[1,8,16,256]{3,2,1,0:T(8,128)(2,1)S(1)}, u32[]{:S(2)}, u32[]{:S(2)}) collective-permute-start(bf16[1,8,16,256]{3,2,1,0:T(8,128)(2,1)S(1)} %get-tuple-element.488), channel_id=1, source_target_pairs={{1,0},{2,1},{3,2},{0,3},{5,4},{6,5},{7,6},{4,7},{9,8},{10,9},{11,1... | collective-permute-start | bytes 196616 | tf_op jit(solution)/shard_map/ppermute | solution.py:21
  54.4 5.2 %all-gather.1 = f32[32,256]{1,0:T(8,128)S(1)} all-gather(f32[8,256]{1,0:T(8,128)S(1)} %convert_reduce_fusion), channel_id=3, replica_groups=mesh['grp'=2,'lat'=4,'lon'=4] {'lon'}, dimensions={0}, use_global_device_ids=true | all-gather | bytes 40960 | tf_op jit(solution)/shard_map/all_gather | solution.py:40
  60.4 15.7 %reduce-scatter.5.cloned.1.call-done = f32[9,256,64]{1,2,0:T(8,128)} async-done(((f32[9,256,256]{1,2,0:T(8,128)}), f32[9,256,64]{1,2,0:T(8,128)}) %reduce-scatter.5.cloned.1.call-update) | async-done | bytes 589840 | tf_op jit(solution)/shard_map/reduce_scatter | solution.py:48
  76.1 2.4 %copy.35 = f32[9,256,64]{2,0,1:T(8,128)S(1)} copy(f32[9,256,64]{1,2,0:T(8,128)} %reduce-scatter.5.cloned.1.call-done) | data formatting | bytes 1179648
  79.8 28.7 %while.27 = (s32[]{:T(128)}, bf16[4,1,64,9,256]{4,2,3,1,0:T(8,128)(2,1)}, s32[4]{0:T(128)S(1)}, s32[8,12]{1,0:T(8,128)S(1)}, s32[8,12]{1,0:T(8,128)S(1)}, /*inde...) while((s32[]{:T(128)}, ...), condition=%wide.region_8.9_spmd.clone.clone, body=%wide.region_6.8_spmd.clone.clone.sunk | while | flops 891077120 | bytes 5929787 | solution.py:144
  83.1 1.6 %fusion.122 = f32[5,9,96,64]{2,1,3,0:T(8,128)S(1)} fusion(s32[5,12]{1,0:T(8,128)S(1)} %get-tuple-element.654, s32[5,12]{1,0:T(8,128)S(1)} %get-tuple-element.655, s32[96,64]{0,1:T(8,128)S(1)} %subtract_bitcast_fusion.2, pred[5,12]{1,0:T(8,128)(4,1)S(1)} %get-tuple-element.656, f32[5,12]{1,0:T(8,128)S(1)} %dynamic-slice_select_fusion.2, ...), kind=kOutput, calls=%fused_computation.52.clone.1 | convolution fusion | flops 41288760 | bytes 1131516 | tf_op jit(solution)/shard_map/while/body/eval_jaxpr/esvw,esk->ekvw/dot_general | solution.py:132
  85.0 2.0 %fusion.125 = bf16[4,1,64,9,256]{4,2,3,1,0:T(8,128)(2,1)} fusion(bf16[4,1,64,9,256]{4,2,3,1,0:T(8,128)(2,1)} %get-tuple-element.717, s32[]{:T(128)} %get-tuple-element.716, f32[5,9,96,64]{2,1,3,0:T(8,128)S(1)} %fusion.122, f32[9,256]{1,0:T(8,128)S(1)} %fusion.124, bf16[1,8,96,256]{3,2,1,0:T(8,128)(2,1)S(1)} %copy-done, s32[]{:T(128)S(6)} %select_n.107), kind=kOutput, calls=%fused_computation.67.clone.1 | convolution fusion | flops 849641472 | bytes 3179012 | tf_op jit(solution)/shard_map/while/body/eval_jaxpr/bevc,ekvw->bwkc/dot_general | solution.py:135
  90.2 1.6 %fusion.122 = f32[5,9,96,64]{2,1,3,0:T(8,128)S(1)} fusion(s32[5,12]{1,0:T(8,128)S(1)} %get-tuple-element.654, s32[5,12]{1,0:T(8,128)S(1)} %get-tuple-element.655, s32[96,64]{0,1:T(8,128)S(1)} %subtract_bitcast_fusion.2, pred[5,12]{1,0:T(8,128)(4,1)S(1)} %get-tuple-element.656, f32[5,12]{1,0:T(8,128)S(1)} %dynamic-slice_select_fusion.2, ...), kind=kOutput, calls=%fused_computation.52.clone.1 | convolution fusion | flops 41288760 | bytes 1131516 | tf_op jit(solution)/shard_map/while/body/eval_jaxpr/esvw,esk->ekvw/dot_general | solution.py:132
  92.2 2.0 %fusion.125 = bf16[4,1,64,9,256]{4,2,3,1,0:T(8,128)(2,1)} fusion(bf16[4,1,64,9,256]{4,2,3,1,0:T(8,128)(2,1)} %get-tuple-element.717, s32[]{:T(128)} %get-tuple-element.716, f32[5,9,96,64]{2,1,3,0:T(8,128)S(1)} %fusion.122, f32[9,256]{1,0:T(8,128)S(1)} %fusion.124, bf16[1,8,96,256]{3,2,1,0:T(8,128)(2,1)S(1)} %copy-done, s32[]{:T(128)S(6)} %select_n.107), kind=kOutput, calls=%fused_computation.67.clone.1 | convolution fusion | flops 849641472 | bytes 3179012 | tf_op jit(solution)/shard_map/while/body/eval_jaxpr/bevc,ekvw->bwkc/dot_general | solution.py:135
  97.4 1.6 %fusion.122 = f32[5,9,96,64]{2,1,3,0:T(8,128)S(1)} fusion(s32[5,12]{1,0:T(8,128)S(1)} %get-tuple-element.654, s32[5,12]{1,0:T(8,128)S(1)} %get-tuple-element.655, s32[96,64]{0,1:T(8,128)S(1)} %subtract_bitcast_fusion.2, pred[5,12]{1,0:T(8,128)(4,1)S(1)} %get-tuple-element.656, f32[5,12]{1,0:T(8,128)S(1)} %dynamic-slice_select_fusion.2, ...), kind=kOutput, calls=%fused_computation.52.clone.1 | convolution fusion | flops 41288760 | bytes 1131516 | tf_op jit(solution)/shard_map/while/body/eval_jaxpr/esvw,esk->ekvw/dot_general | solution.py:132
  99.3 2.0 %fusion.125 = bf16[4,1,64,9,256]{4,2,3,1,0:T(8,128)(2,1)} fusion(bf16[4,1,64,9,256]{4,2,3,1,0:T(8,128)(2,1)} %get-tuple-element.717, s32[]{:T(128)} %get-tuple-element.716, f32[5,9,96,64]{2,1,3,0:T(8,128)S(1)} %fusion.122, f32[9,256]{1,0:T(8,128)S(1)} %fusion.124, bf16[1,8,96,256]{3,2,1,0:T(8,128)(2,1)S(1)} %copy-done, s32[]{:T(128)S(6)} %select_n.107), kind=kOutput, calls=%fused_computation.67.clone.1 | convolution fusion | flops 849641472 | bytes 3179012 | tf_op jit(solution)/shard_map/while/body/eval_jaxpr/bevc,ekvw->bwkc/dot_general | solution.py:135
  104.6 1.6 %fusion.122 = f32[5,9,96,64]{2,1,3,0:T(8,128)S(1)} fusion(s32[5,12]{1,0:T(8,128)S(1)} %get-tuple-element.654, s32[5,12]{1,0:T(8,128)S(1)} %get-tuple-element.655, s32[96,64]{0,1:T(8,128)S(1)} %subtract_bitcast_fusion.2, pred[5,12]{1,0:T(8,128)(4,1)S(1)} %get-tuple-element.656, f32[5,12]{1,0:T(8,128)S(1)} %dynamic-slice_select_fusion.2, ...), kind=kOutput, calls=%fused_computation.52.clone.1 | convolution fusion | flops 41288760 | bytes 1131516 | tf_op jit(solution)/shard_map/while/body/eval_jaxpr/esvw,esk->ekvw/dot_general | solution.py:132
  106.5 2.0 %fusion.125 = bf16[4,1,64,9,256]{4,2,3,1,0:T(8,128)(2,1)} fusion(bf16[4,1,64,9,256]{4,2,3,1,0:T(8,128)(2,1)} %get-tuple-element.717, s32[]{:T(128)} %get-tuple-element.716, f32[5,9,96,64]{2,1,3,0:T(8,128)S(1)} %fusion.122, f32[9,256]{1,0:T(8,128)S(1)} %fusion.124, bf16[1,8,96,256]{3,2,1,0:T(8,128)(2,1)S(1)} %copy-done, s32[]{:T(128)S(6)} %select_n.107), kind=kOutput, calls=%fused_computation.67.clone.1 | convolution fusion | flops 849641472 | bytes 3179012 | tf_op jit(solution)/shard_map/while/body/eval_jaxpr/bevc,ekvw->bwkc/dot_general | solution.py:135
  108.5 2.0 %copy.28 = bf16[4,1,64,9,256]{4,3,2,0,1:T(8,128)(2,1)S(1)} copy(bf16[4,1,64,9,256]{4,2,3,1,0:T(8,128)(2,1)} %get-tuple-element.253) | data formatting | bytes 2359296 | tf_op jit(solution)/shard_map/while | solution.py:144
  110.6 1.5 %reshape.376 = bf16[4,64,2304]{2,1,0:T(8,128)(2,1)} reshape(bf16[4,1,64,9,256]{4,3,2,0,1:T(8,128)(2,1)S(1)} %copy.28) | data formatting | bytes 2359296 | tf_op jit(solution)/shard_map/reshape.32
  112.1 2.6 %convolution_bitcast_fusion.2 = f32[1,4,64,256]{3,2,1,0:T(8,128)} fusion(bf16[4,64,2304]{2,1,0:T(8,128)(2,1)S(1)} %reshape.374, bf16[2304,256,1]{1,0,2:T(8,128)(2,1)} %bitcast.169), kind=kOutput, calls=%fused_computation.95 | convolution fusion | flops 301989888 | bytes 2621440 | tf_op jit(solution)/shard_map/rbwq,qo->brwo/dot_general | solution.py:88
  (156 shorter events, 27.5 us)
Async XLA Ops:
  7.2 19.2 %copy-start.5 = (s32[16,12]{1,0:T(8,128)S(1)}, s32[16,12]{1,0:T(8,128)}, u32[]{:S(2)}) copy-start(s32[16,12]{1,0:T(8,128)} %param.17) | copy-start | bytes 2308
  7.2 19.2 %copy-start.6 = (s32[16,12]{1,0:T(8,128)S(1)}, s32[16,12]{1,0:T(8,128)}, u32[]{:S(2)}) copy-start(s32[16,12]{1,0:T(8,128)} %param.15) | copy-start | bytes 2308
  7.2 19.2 %copy-start.8 = (s32[16,12]{1,0:T(8,128)S(1)}, s32[16,12]{1,0:T(8,128)}, u32[]{:S(2)}) copy-start(s32[16,12]{1,0:T(8,128)} %param.18) | copy-start | bytes 2308
  7.2 19.2 %copy-start.7 = (s32[16,12]{1,0:T(8,128)S(1)}, s32[16,12]{1,0:T(8,128)}, u32[]{:S(2)}) copy-start(s32[16,12]{1,0:T(8,128)} %param.16) | copy-start | bytes 2308
  7.2 68.9 %reduce-scatter.5.cloned.1.call-start = ((), (), s32[]{:S(2)}) async-start(), calls=%async_computation.2 | async-start | bytes 2949120 | tf_op jit(solution)/shard_map/reduce_scatter | solution.py:48
  8.1 7.0 %collective-permute-start = (bf16[1,2,64,256]{3,2,1,0:T(8,128)(2,1)S(1)}, bf16[1,2,64,256]{3,2,1,0:T(8,128)(2,1)S(1)}, u32[]{:S(2)}, u32[]{:S(2)}) collective-permute-start(bf16[1,2,64,256]{3,2,1,0:T(8,128)(2,1)S(1)} %get-tuple-element.494), channel_id=1, source_target_pairs={{0,4},{4,8},{8,12},{1,5},{5,9},{9,13},{2,6},{6,10},{10,14},{3,7},{... | collective-permute-start | bytes 196616 | tf_op jit(solution)/shard_map/ppermute | solution.py:18
  13.1 6.2 %collective-permute-start.1 = (bf16[1,2,64,256]{3,2,1,0:T(8,128)(2,1)S(1)}, bf16[1,2,64,256]{3,2,1,0:T(8,128)(2,1)S(1)}, u32[]{:S(2)}, u32[]{:S(2)}) collective-permute-start(bf16[1,2,64,256]{3,2,1,0:T(8,128)(2,1)S(1)} %get-tuple-element.493), channel_id=1, source_target_pairs={{4,0},{8,4},{12,8},{5,1},{9,5},{13,9},{6,2},{10,6},{14,10},{7,3},{... | collective-permute-start | bytes 196616 | tf_op jit(solution)/shard_map/ppermute | solution.py:21
  19.3 7.0 %collective-permute-start.2 = (bf16[1,8,16,256]{3,2,1,0:T(8,128)(2,1)S(1)}, bf16[1,8,16,256]{3,2,1,0:T(8,128)(2,1)S(1)}, u32[]{:S(2)}, u32[]{:S(2)}) collective-permute-start(bf16[1,8,16,256]{3,2,1,0:T(8,128)(2,1)S(1)} %get-tuple-element.489), channel_id=1, source_target_pairs={{0,1},{1,2},{2,3},{3,0},{4,5},{5,6},{6,7},{7,4},{8,9},{9,10},{10,1... | collective-permute-start | bytes 196616 | tf_op jit(solution)/shard_map/ppermute | solution.py:18
  19.4 6.9 %collective-permute-start.3 = (bf16[1,8,16,256]{3,2,1,0:T(8,128)(2,1)S(1)}, bf16[1,8,16,256]{3,2,1,0:T(8,128)(2,1)S(1)}, u32[]{:S(2)}, u32[]{:S(2)}) collective-permute-start(bf16[1,8,16,256]{3,2,1,0:T(8,128)(2,1)S(1)} %get-tuple-element.490), channel_id=1, source_target_pairs={{1,0},{2,1},{3,2},{0,3},{5,4},{6,5},{7,6},{4,7},{9,8},{10,9},{11,1... | collective-permute-start | bytes 196616 | tf_op jit(solution)/shard_map/ppermute | solution.py:21
  39.8 0.9 copy-start.4
  42.6 5.0 %copy-start.2 = (bf16[9,256,256]{2,1,0:T(8,128)(2,1)S(1)}, bf16[9,256,256]{2,1,0:T(8,128)(2,1)}, u32[]{:S(2)}) copy-start(bf16[9,256,256]{2,1,0:T(8,128)(2,1)} %param.14) | copy-start | bytes 3538948
  42.6 73.2 %reduce-scatter.7.cloned.1.call-start = ((), (), s32[]{:S(2)}) async-start(), calls=%async_computation.3 | async-start | bytes 819200
  42.7 6.5 %collective-permute-start.4 = (bf16[1,2,64,256]{3,2,1,0:T(8,128)(2,1)S(1)}, bf16[1,2,64,256]{3,2,1,0:T(8,128)(2,1)S(1)}, u32[]{:S(2)}, u32[]{:S(2)}) collective-permute-start(bf16[1,2,64,256]{3,2,1,0:T(8,128)(2,1)S(1)} %get-tuple-element.492), channel_id=1, source_target_pairs={{0,4},{4,8},{8,12},{1,5},{5,9},{9,13},{2,6},{6,10},{10,14},{3,7},{... | collective-permute-start | bytes 196616 | tf_op jit(solution)/shard_map/ppermute | solution.py:18
  46.3 6.2 %collective-permute-start.5 = (bf16[1,2,64,256]{3,2,1,0:T(8,128)(2,1)S(1)}, bf16[1,2,64,256]{3,2,1,0:T(8,128)(2,1)S(1)}, u32[]{:S(2)}, u32[]{:S(2)}) collective-permute-start(bf16[1,2,64,256]{3,2,1,0:T(8,128)(2,1)S(1)} %get-tuple-element.491), channel_id=1, source_target_pairs={{4,0},{8,4},{12,8},{5,1},{9,5},{13,9},{6,2},{10,6},{14,10},{7,3},{... | collective-permute-start | bytes 196616 | tf_op jit(solution)/shard_map/ppermute | solution.py:21
  52.5 7.1 %collective-permute-start.6 = (bf16[1,8,16,256]{3,2,1,0:T(8,128)(2,1)S(1)}, bf16[1,8,16,256]{3,2,1,0:T(8,128)(2,1)S(1)}, u32[]{:S(2)}, u32[]{:S(2)}) collective-permute-start(bf16[1,8,16,256]{3,2,1,0:T(8,128)(2,1)S(1)} %get-tuple-element.487), channel_id=1, source_target_pairs={{0,1},{1,2},{2,3},{3,0},{4,5},{5,6},{6,7},{7,4},{8,9},{9,10},{10,1... | collective-permute-start | bytes 196616 | tf_op jit(solution)/shard_map/ppermute | solution.py:18
  52.6 7.0 %collective-permute-start.7 = (bf16[1,8,16,256]{3,2,1,0:T(8,128)(2,1)S(1)}, bf16[1,8,16,256]{3,2,1,0:T(8,128)(2,1)S(1)}, u32[]{:S(2)}, u32[]{:S(2)}) collective-permute-start(bf16[1,8,16,256]{3,2,1,0:T(8,128)(2,1)S(1)} %get-tuple-element.488), channel_id=1, source_target_pairs={{1,0},{2,1},{3,2},{0,3},{5,4},{6,5},{7,6},{4,7},{9,8},{10,9},{11,1... | collective-permute-start | bytes 196616 | tf_op jit(solution)/shard_map/ppermute | solution.py:21
  83.1 1.9 %copy-start = (bf16[1,8,96,256]{3,2,1,0:T(8,128)(2,1)S(1)}, bf16[1,8,96,256]{3,2,1,0:T(8,128)(2,1)}, u32[]{:S(2)}) copy-start(bf16[1,8,96,256]{3,2,1,0:T(8,128)(2,1)} %get-tuple-element.740) | copy-start | bytes 1179652 | tf_op jit(solution)/shard_map/while
  90.2 1.9 %copy-start = (bf16[1,8,96,256]{3,2,1,0:T(8,128)(2,1)S(1)}, bf16[1,8,96,256]{3,2,1,0:T(8,128)(2,1)}, u32[]{:S(2)}) copy-start(bf16[1,8,96,256]{3,2,1,0:T(8,128)(2,1)} %get-tuple-element.740) | copy-start | bytes 1179652 | tf_op jit(solution)/shard_map/while
  97.4 1.9 %copy-start = (bf16[1,8,96,256]{3,2,1,0:T(8,128)(2,1)S(1)}, bf16[1,8,96,256]{3,2,1,0:T(8,128)(2,1)}, u32[]{:S(2)}) copy-start(bf16[1,8,96,256]{3,2,1,0:T(8,128)(2,1)} %get-tuple-element.740) | copy-start | bytes 1179652 | tf_op jit(solution)/shard_map/while
  104.6 1.9 %copy-start = (bf16[1,8,96,256]{3,2,1,0:T(8,128)(2,1)S(1)}, bf16[1,8,96,256]{3,2,1,0:T(8,128)(2,1)}, u32[]{:S(2)}) copy-start(bf16[1,8,96,256]{3,2,1,0:T(8,128)(2,1)} %get-tuple-element.740) | copy-start | bytes 1179652 | tf_op jit(solution)/shard_map/while
  112.1 2.6 %copy-start.1 = (bf16[4,64,2304]{2,1,0:T(8,128)(2,1)S(1)}, bf16[4,64,2304]{2,1,0:T(8,128)(2,1)}, u32[]{:S(2)}) copy-start(bf16[4,64,2304]{2,1,0:T(8,128)(2,1)} %reshape.376) | copy-start | bytes 3538948
  112.1 2.6 %copy-start.3 = (bf16[9,256,256]{1,2,0:T(8,128)(2,1)S(1)}, bf16[9,256,256]{1,2,0:T(8,128)(2,1)}, u32[]{:S(2)}) copy-start(bf16[9,256,256]{1,2,0:T(8,128)(2,1)} %copy.29) | copy-start | bytes 3538948
Sparse Core Ops, SparseCore 0:
  42.8 33.2 reduce-scatter.4
  79.9 22.1 reduce-scatter.6
